TPU v7x, 32 devices: a whole 2x2x4 slice. The times are simulated.
32 devices in a mesh: expert: 8 (over z, x), rep: 4 (over y, core).
Axes of the slice: x: 2, y: 2, z: 4, core: 2. Of those that a mesh axis runs over, the one named last changes fastest.
Arguments:
- tokens: bfloat16 [4, 2048, 2, 2048], P('rep', 'expert'), may hold values from -6 to 6
- expert_ids: int32 [4, 2048, 2, 2], P('rep', 'expert'), may hold values from 0 to 15, all different within a row; in each aligned block of 512 rows (0 to 511, 512 to 1023, ..., all dimensions but the last counted through in order) at most 80 rows name the same one
- gate_probs: float32 [4, 2048, 2, 2], P('rep', 'expert'), may hold values from 0.1 to 1
- norm_gain: float32 [2048], replicated, may hold values from 0.25 to 1.75
- expert_gate: bfloat16 [16, 2048, 1408], P('expert', None, 'rep'), may hold values from -0.125 to 0.125
- expert_up: bfloat16 [16, 2048, 1408], P('expert', None, 'rep'), may hold values from -0.125 to 0.125
- expert_down: bfloat16 [16, 1408, 2048], P('expert', 'rep'), may hold values from -0.15625 to 0.15625
- teacher_gain: float32 [2048], replicated, may hold values from 0.25 to 1.75
- teacher_qkv: bfloat16 [2048, 3, 16, 128], P(None, None, 'rep')
- qk_gain: float32 [2, 16, 128], P(None, 'rep'), may hold values from 0.5 to 7.5
- teacher_out: bfloat16 [16, 128, 2048], P('rep'), may hold values from -0.125 to 0.125
- critic_in: bfloat16 [2048, 1024], replicated, may hold values from -0.125 to 0.125
- critic_out: float32 [1024], replicated, may hold values from -0.1875 to 0.1875
Outputs:
- teacher_features: bfloat16 [4, 2048, 2, 2048], P('rep', 'expert')
- critic_logits: float32 [4, 2048, 2], P('rep', 'expert')
Inputs may be any that keep to these rules, and one draw needn't show every extreme that they name: `expert_ids`: the 512 rows of one device name one expert at most 80 times in all, and some device reaches 80; the two experts of a token differ.
All inputs are finite; a program needn't handle non-finite values.
Results may differ from a plain program's by a relative error of at most 0.033.
Values may be sent and summed in bfloat16 or wider, within the bound.
No kernel may reach another device: no remote copies, remote signals or barrier semaphores. Data moves between devices by JAX's collectives and lax.ppermute only.
A program may use at most 192 MiB of HBM per device.

v0:
```python
import jax
import jax.numpy as jnp
from jax import lax
from jax.sharding import PartitionSpec as P


def norm_rows(values, gain):
    return values * lax.rsqrt(jnp.mean(values * values, axis=-1, keepdims=True) + 1e-06) * gain


def slot_numbers(chosen, count):
    onehot = (chosen[..., None] == jnp.arange(count, dtype=jnp.int32)).astype(jnp.int32)
    before = jnp.cumsum(onehot, axis=-2) - onehot
    return jnp.sum(before * onehot, axis=-1)


def local(
    tokens,
    expert_ids,
    gate_probs,
    norm_gain,
    expert_gate,
    expert_up,
    expert_down,
    teacher_gain,
    teacher_qkv,
    qk_gain,
    teacher_out,
    critic_in,
    critic_out,
):
    seq_dev = tokens.shape[1]
    images = tokens.shape[2]
    width = tokens.shape[3]
    tok_count = seq_dev * images
    n_owner = lax.axis_size("expert")
    n_replica = lax.axis_size("rep")
    exp_local = expert_gate.shape[0]
    expert_total = exp_local * n_owner
    capacity = max(2, tok_count * 10 // (4 * expert_total))
    gate_full = lax.all_gather(expert_gate, "rep", axis=2, tiled=True)
    up_full = lax.all_gather(expert_up, "rep", axis=2, tiled=True)
    down_full = lax.all_gather(expert_down, "rep", axis=1, tiled=True)
    qkv_full = lax.all_gather(teacher_qkv, "rep", axis=2, tiled=True)
    qk_gain_full = lax.all_gather(qk_gain, "rep", axis=1, tiled=True)
    out_full = lax.all_gather(teacher_out, "rep", axis=0, tiled=True)
    residual = tokens.reshape(tok_count, width).astype(jnp.float32)
    normed = norm_rows(residual, norm_gain).astype(jnp.bfloat16)
    chosen = expert_ids.reshape(2 * tok_count)
    slot_index = slot_numbers(chosen, expert_total)
    gate_value = gate_probs.reshape(2 * tok_count)
    target = chosen * capacity + slot_index
    token_of = jnp.arange(2 * tok_count, dtype=jnp.int32) // 2
    owner_token = jnp.zeros((expert_total * capacity,), jnp.int32).at[target].set(token_of)
    filled = jnp.zeros((expert_total * capacity,), jnp.bool_).at[target].set(True)
    outgoing = jnp.where(
        filled[:, None], jnp.take(normed, owner_token, axis=0), jnp.zeros((), jnp.bfloat16)
    )
    outgoing = outgoing.reshape(n_owner, exp_local * capacity, width)
    arrived = lax.all_to_all(outgoing, "expert", split_axis=0, concat_axis=0, tiled=True)
    arrived = arrived.reshape(n_owner, exp_local, capacity, width)
    gate_part = jnp.einsum("sjcd,jdf->sjcf", arrived, gate_full, preferred_element_type=jnp.float32)
    up_part = jnp.einsum("sjcd,jdf->sjcf", arrived, up_full, preferred_element_type=jnp.float32)
    hidden = (jax.nn.silu(gate_part) * up_part).astype(jnp.bfloat16)
    ff_total = hidden.shape[-1]
    ff_part = ff_total // n_replica
    produced = jnp.zeros(arrived.shape, jnp.float32)
    for part in range(n_replica):
        low = part * ff_part
        produced = produced + jnp.einsum(
            "sjcf,jfd->sjcd",
            hidden[..., low : low + ff_part],
            down_full[:, low : low + ff_part],
            preferred_element_type=jnp.float32,
        ).astype(jnp.bfloat16).astype(jnp.float32)
    results = produced.astype(jnp.bfloat16).reshape(n_owner, exp_local * capacity, width)
    returned = lax.all_to_all(results, "expert", split_axis=0, concat_axis=0, tiled=True).reshape(
        expert_total * capacity, width
    )
    picked = jnp.take(returned, target, axis=0).astype(jnp.float32) * gate_value[:, None]
    combined = picked.reshape(tok_count, 2, width).sum(axis=1)
    mixed = (residual + combined).astype(jnp.bfloat16)
    teacher_in = norm_rows(mixed.astype(jnp.float32), teacher_gain).astype(jnp.bfloat16)
    teacher_in = teacher_in.reshape(seq_dev, images, width)
    heads_all = qkv_full.shape[2]
    head_size = qkv_full.shape[3]
    projected = jnp.einsum(
        "sid,djhe->jihse", teacher_in, qkv_full, preferred_element_type=jnp.float32
    )
    query = norm_rows(projected[0], qk_gain_full[0][:, None, :])
    keyed = norm_rows(projected[1], qk_gain_full[1][:, None, :])
    projected = jnp.stack([query, keyed, projected[2]]).astype(jnp.bfloat16)
    pairs_all = images * heads_all
    grouped = projected.reshape(3, pairs_all, seq_dev, head_size)
    whole = lax.all_to_all(grouped, "expert", split_axis=1, concat_axis=2, tiled=True)
    pairs_local = whole.shape[1]
    seq_len = whole.shape[2]
    block = min(512, seq_len)
    blocks_count = seq_len // block
    key_rows = whole[1]
    value_rows = whole[2]

    def attend(query_block):
        scores = jnp.einsum(
            "pqe,pke->pqk", query_block, key_rows, preferred_element_type=jnp.float32
        ) * head_size ** (-0.5)
        scores = scores - jnp.max(scores, axis=-1, keepdims=True)
        weights = jnp.exp(scores)
        probs = (weights / jnp.sum(weights, axis=-1, keepdims=True)).astype(jnp.bfloat16)
        return jnp.einsum(
            "pqk,pke->pqe", probs, value_rows, preferred_element_type=jnp.float32
        ).astype(jnp.bfloat16)

    query_blocks = (
        whole[0].reshape(pairs_local, blocks_count, block, head_size).transpose(1, 0, 2, 3)
    )
    attended = (
        lax.map(attend, query_blocks).transpose(1, 0, 2, 3).reshape(pairs_local, seq_len, head_size)
    )
    gathered_heads = lax.all_to_all(attended, "expert", split_axis=1, concat_axis=0, tiled=True)
    gathered_heads = gathered_heads.reshape(images, heads_all, seq_dev, head_size)
    heads_part = heads_all // n_replica
    projected_out = jnp.zeros((seq_dev, images, width), jnp.float32)
    for part in range(n_replica):
        low = part * heads_part
        projected_out = projected_out + jnp.einsum(
            "ihse,hed->sid",
            gathered_heads[:, low : low + heads_part],
            out_full[low : low + heads_part],
            preferred_element_type=jnp.float32,
        ).astype(jnp.bfloat16).astype(jnp.float32)
    features = (mixed.reshape(seq_dev, images, width).astype(jnp.float32) + projected_out).astype(
        jnp.bfloat16
    )
    critic_hidden = jax.nn.gelu(
        jnp.dot(features.reshape(tok_count, width), critic_in, preferred_element_type=jnp.float32),
        approximate=True,
    )
    logits = jnp.dot(
        critic_hidden,
        critic_out,
        precision=lax.Precision.HIGHEST,
        preferred_element_type=jnp.float32,
    )
    return (features.reshape(1, seq_dev, images, width), logits.reshape(1, seq_dev, images))


def solution(mesh):
    return jax.shard_map(
        local,
        mesh=mesh,
        in_specs=(
            P("rep", "expert", None, None),
            P("rep", "expert", None, None),
            P("rep", "expert", None, None),
            P(),
            P("expert", None, "rep"),
            P("expert", None, "rep"),
            P("expert", "rep", None),
            P(),
            P(None, None, "rep", None),
            P(None, "rep", None),
            P("rep", None, None),
            P(),
            P(),
        ),
        out_specs=(P("rep", "expert", None, None), P("rep", "expert", None)),
        check_vma=False,
    )
```

profile of v0, /device:TPU:0, one launch (start us, length us, event | category | flops | bytes accessed | tf_op | source)
XLA Modules:
  0.0 909.0 jit_solution(2036090906852341895)
XLA Ops:
  9.4 10.8 %copy.124 = bf16[2048,3,4,128]{0,3,2,1:T(8,128)(2,1)} copy(bf16[2048,3,4,128]{3,2,1,0:T(4,128)(2,1)} %param.23) | data formatting | bytes 12582912 | tf_op args[8]
  21.7 4.5 reduce-window.6
  28.1 5.3 copy.115
  33.3 6.1 reshape.216
  41.1 4.8 scatter_custom_fusion.1
  46.1 4.3 scatter_custom_fusion
  50.5 2.6 multiply_convert_fusion.2
  53.1 6.1 gather_fusion
  59.3 3.7 select_select_fusion
  63.0 123.0 %all_to_all.40 = bf16[8,160,2048]{2,1,0:T(8,128)(2,1)} all-to-all(bf16[8,160,2048]{2,1,0:T(8,128)(2,1)S(1)} %select_select_fusion), channel_id=1, replica_groups=mesh['expert'=8,'rep'=4] {'expert'}, dimensions={0} | all-to-all | bytes 10485760 | tf_op jit(solution)/shard_map/all_to_all | solution.py:60
  186.0 14.7 %fusion.23 = f32[2,8,80,1408]{3,2,1,0:T(8,128)} fusion(bf16[2,2048,1408]{1,2,0:T(8,128)(2,1)} %all-gather.8.cloned.1.call-done, bf16[8,2,80,2048]{3,2,1,0:T(8,128)(2,1)} %bitcast.207), kind=kOutput, calls=%fused_computation.23 | convolution fusion | flops 7381975040 | bytes 23986176 | tf_op jit(solution)/shard_map/sjcd,jdf->sjcf/dot_general | solution.py:63
  200.7 16.6 %fusion.27 = bf16[8,2,80,1408]{3,2,0,1:T(8,128)(2,1)} fusion(f32[2,8,80,1408]{3,2,1,0:T(8,128)} %fusion.23, bf16[2,2048,1408]{1,2,0:T(8,128)(2,1)} %all-gather.6.cloned.1.call-done, bf16[8,2,80,2048]{3,2,1,0:T(8,128)(2,1)} %bitcast.208), kind=kOutput, calls=%fused_computation.31 | convolution fusion | flops 7392788480 | bytes 27590656 | tf_op jit(solution)/shard_map/sjcd,jdf->sjcf/dot_general | solution.py:62
  217.3 26.6 %all-gather.10.cloned.1.call-done = bf16[2,1408,2048]{2,1,0:T(8,128)(2,1)} async-done(((bf16[2,352,2048]{2,1,0:T(8,128)(2,1)}), bf16[2,1408,2048]{2,1,0:T(8,128)(2,1)}) %all-gather.10.cloned.1.call-update) | async-done | bytes 11534352 | tf_op jit(solution)/shard_map/all_gather | solution.py:43
  243.9 5.3 fusion.45
  249.2 6.8 fusion.46
  256.0 7.8 fusion.44
  263.8 9.1 fusion.31
  272.9 2.9 copy.119
  275.8 5.7 all-to-all-start.1
  282.6 5.4 all_gather.22
  288.0 109.6 %all-to-all-done.1 = bf16[8,160,2048]{2,1,0:T(8,128)(2,1)} async-done(((bf16[8,160,2048]{2,1,0:T(8,128)(2,1)}), bf16[8,160,2048]{2,1,0:T(8,128)(2,1)}, u32[]{:S(2)}, u32[]{:S(2)}) %all-to-all-start.1) | async-done | bytes 5242912 | tf_op jit(solution)/shard_map/all_to_all | solution.py:77
  397.7 12.3 %gather_fusion.1 = bf16[1024,2048]{1,0:T(8,128)(2,1)} fusion(bf16[1280,2048]{1,0:T(8,128)(2,1)} %bitcast.25, s32[1024]{0:T(1024)S(1)} %broadcast_clamp_fusion), kind=kCustom, calls=%fused_computation.1 | custom fusion | bytes 8392704 | tf_op jit(solution)/shard_map/jit(_take)/gather | solution.py:80
  409.9 7.6 gather.15
  417.6 20.7 %multiply_reduce_fusion.1 = f32[512,2048]{1,0:T(8,128)} fusion(bf16[512,2,2048]{2,1,0:T(2,128)(2,1)} %gather.15, pred[512,2]{1,0:T(8,128)(4,1)S(1)} %copy.113, f32[512,2]{1,0:T(8,128)S(1)} %bitcast.215), kind=kLoop, calls=%fused_computation.28 | loop fusion | flops 7340032 | bytes 8393728 | tf_op jit(solution)/shard_map/reduce_sum | solution.py:81
  438.2 5.8 reduce_sum.77
  444.1 6.0 reduce_sum.76
  450.1 5.6 multiply_reduce_fusion.4
  455.7 26.6 %fusion.36 = f32[3,2,16,256,128]{3,4,2,0,1:T(8,128)} fusion(bf16[2048,3,16,128]{0,3,2,1:T(8,128)(2,1)} %all-gather.12.cloned.1.call-done, f32[2048]{0:T(1024)S(1)} %copy-done.12, f32[256,2]{0,1:T(2,128)S(1)} %add_rsqrt_fusion.2, f32[256,2,2048]{2,1,0:T(2,128)} %reduce_sum.76, bf16[1,256,2,2048]{3,2,1,0:T(2,128)(2,1)S(1)} %copy-done.2), kind=kOutput, calls=%fused_computation.44 | convolution fusion | flops 12892241920 | bytes 44050432 | tf_op jit(solution)/shard_map/sid,djhe->jihse/dot_general | solution.py:87
  482.3 4.8 multiply_reduce_fusion.3
  487.2 3.2 slice.165
  490.6 2.7 multiply_convert_fusion.1
  493.3 4.0 copy.126
  497.3 4.1 copy.127
  501.4 2.8 copy.128
  504.3 6.4 pad_maximum_fusion
  510.7 4.9 all-to-all-start.2
  516.2 137.0 %all-to-all-done.2 = bf16[3,32,256,128]{3,2,0,1:T(8,128)(2,1)} async-done(((bf16[3,32,256,128]{3,2,0,1:T(8,128)(2,1)}), bf16[3,32,256,128]{3,2,0,1:T(8,128)(2,1)}, u32[]{:S(2)}, u32[]{:S(2)}) %all-to-all-start.2) | async-done | bytes 6291488 | tf_op jit(solution)/shard_map/all_to_all | solution.py:95
  653.2 3.2 copy.129
  656.9 1.6 copy.130
  658.6 1.5 copy.132
  660.1 152.0 %while.10 = (s32[]{:T(128)}, bf16[4,4,512,128]{3,2,0,1:T(8,128)(2,1)}, bf16[4,4,512,128]{3,2,0,1:T(8,128)(2,1)}, bf16[4,2048,128]{2,1,0:T(8,128)(2,1)S(1)}, bf16[4,2048,128]{2,1,0:T(8,128)(2,1)}, /*index=5*/s32[]{:T(128)}) while((s32[]{:T(128)}, bf16[4,4,512,128]{3,2,0,1:T(8,128)(2,1)}, bf16[4,4,512,128]{3,2,0,1:T(8,128)(2,1)}, ...), condition=%wide.region_13.14_spmd, body=%wide.region_10.13_spmd.sunk | while | flops 2185500672 | bytes 72369224 | solution.py:118
  660.2 9.1 %fusion.110 = f32[4,512,2048]{2,1,0:T(8,128)} fusion(bf16[4,2048,128]{2,1,0:T(8,128)(2,1)S(1)} %get-tuple-element.127, bf16[4,4,512,128]{3,2,0,1:T(8,128)(2,1)} %get-tuple-element.126, s32[]{:T(128)} %get-tuple-element.118), kind=kOutput, calls=%fused_computation.14.clone.1 | convolution fusion | flops 1073741824 | bytes 19399168 | tf_op jit(solution)/shard_map/while/body/eval_jaxpr/pqe,pke->pqk/dot_general | solution.py:104
  669.3 14.1 %fusion.111 = f32[4,512]{1,0:T(4,128)S(1)} fusion(f32[4,512,2048]{2,1,0:T(8,128)} %fusion.110), kind=kOutput, calls=%fused_computation.135.clone.1 | output fusion | flops 16779264 | bytes 16785408 | tf_op jit(solution)/shard_map/while/body/eval_jaxpr/sub | solution.py:107
  683.4 14.7 %fusion.112 = bf16[4,4,512,128]{3,2,0,1:T(8,128)(2,1)} fusion(bf16[4,4,512,128]{3,2,0,1:T(8,128)(2,1)} %get-tuple-element.119, s32[]{:T(128)} %get-tuple-element.118, bf16[4,2048,128]{2,1,0:T(8,128)(2,1)} %get-tuple-element.128, f32[4,512]{1,0:T(4,128)S(1)} %fusion.111, f32[4,512,2048]{2,1,0:T(8,128)} %fusion.110), kind=kOutput, calls=%fused_computation.13.clone.1 | convolution fusion | flops 1094979584 | bytes 36184576 | tf_op jit(solution)/shard_map/while/body/eval_jaxpr/pqk,pke->pqe/dot_general | solution.py:110
  698.2 9.1 %fusion.110 = f32[4,512,2048]{2,1,0:T(8,128)} fusion(bf16[4,2048,128]{2,1,0:T(8,128)(2,1)S(1)} %get-tuple-element.127, bf16[4,4,512,128]{3,2,0,1:T(8,128)(2,1)} %get-tuple-element.126, s32[]{:T(128)} %get-tuple-element.118), kind=kOutput, calls=%fused_computation.14.clone.1 | convolution fusion | flops 1073741824 | bytes 19399168 | tf_op jit(solution)/shard_map/while/body/eval_jaxpr/pqe,pke->pqk/dot_general | solution.py:104
  707.3 14.1 %fusion.111 = f32[4,512]{1,0:T(4,128)S(1)} fusion(f32[4,512,2048]{2,1,0:T(8,128)} %fusion.110), kind=kOutput, calls=%fused_computation.135.clone.1 | output fusion | flops 16779264 | bytes 16785408 | tf_op jit(solution)/shard_map/while/body/eval_jaxpr/sub | solution.py:107
  721.4 14.7 %fusion.112 = bf16[4,4,512,128]{3,2,0,1:T(8,128)(2,1)} fusion(bf16[4,4,512,128]{3,2,0,1:T(8,128)(2,1)} %get-tuple-element.119, s32[]{:T(128)} %get-tuple-element.118, bf16[4,2048,128]{2,1,0:T(8,128)(2,1)} %get-tuple-element.128, f32[4,512]{1,0:T(4,128)S(1)} %fusion.111, f32[4,512,2048]{2,1,0:T(8,128)} %fusion.110), kind=kOutput, calls=%fused_computation.13.clone.1 | convolution fusion | flops 1094979584 | bytes 36184576 | tf_op jit(solution)/shard_map/while/body/eval_jaxpr/pqk,pke->pqe/dot_general | solution.py:110
  736.2 9.1 %fusion.110 = f32[4,512,2048]{2,1,0:T(8,128)} fusion(bf16[4,2048,128]{2,1,0:T(8,128)(2,1)S(1)} %get-tuple-element.127, bf16[4,4,512,128]{3,2,0,1:T(8,128)(2,1)} %get-tuple-element.126, s32[]{:T(128)} %get-tuple-element.118), kind=kOutput, calls=%fused_computation.14.clone.1 | convolution fusion | flops 1073741824 | bytes 19399168 | tf_op jit(solution)/shard_map/while/body/eval_jaxpr/pqe,pke->pqk/dot_general | solution.py:104
  745.3 14.1 %fusion.111 = f32[4,512]{1,0:T(4,128)S(1)} fusion(f32[4,512,2048]{2,1,0:T(8,128)} %fusion.110), kind=kOutput, calls=%fused_computation.135.clone.1 | output fusion | flops 16779264 | bytes 16785408 | tf_op jit(solution)/shard_map/while/body/eval_jaxpr/sub | solution.py:107
  759.4 14.7 %fusion.112 = bf16[4,4,512,128]{3,2,0,1:T(8,128)(2,1)} fusion(bf16[4,4,512,128]{3,2,0,1:T(8,128)(2,1)} %get-tuple-element.119, s32[]{:T(128)} %get-tuple-element.118, bf16[4,2048,128]{2,1,0:T(8,128)(2,1)} %get-tuple-element.128, f32[4,512]{1,0:T(4,128)S(1)} %fusion.111, f32[4,512,2048]{2,1,0:T(8,128)} %fusion.110), kind=kOutput, calls=%fused_computation.13.clone.1 | convolution fusion | flops 1094979584 | bytes 36184576 | tf_op jit(solution)/shard_map/while/body/eval_jaxpr/pqk,pke->pqe/dot_general | solution.py:110
  774.2 9.1 %fusion.110 = f32[4,512,2048]{2,1,0:T(8,128)} fusion(bf16[4,2048,128]{2,1,0:T(8,128)(2,1)S(1)} %get-tuple-element.127, bf16[4,4,512,128]{3,2,0,1:T(8,128)(2,1)} %get-tuple-element.126, s32[]{:T(128)} %get-tuple-element.118), kind=kOutput, calls=%fused_computation.14.clone.1 | convolution fusion | flops 1073741824 | bytes 19399168 | tf_op jit(solution)/shard_map/while/body/eval_jaxpr/pqe,pke->pqk/dot_general | solution.py:104
  783.3 14.1 %fusion.111 = f32[4,512]{1,0:T(4,128)S(1)} fusion(f32[4,512,2048]{2,1,0:T(8,128)} %fusion.110), kind=kOutput, calls=%fused_computation.135.clone.1 | output fusion | flops 16779264 | bytes 16785408 | tf_op jit(solution)/shard_map/while/body/eval_jaxpr/sub | solution.py:107
  797.4 14.7 %fusion.112 = bf16[4,4,512,128]{3,2,0,1:T(8,128)(2,1)} fusion(bf16[4,4,512,128]{3,2,0,1:T(8,128)(2,1)} %get-tuple-element.119, s32[]{:T(128)} %get-tuple-element.118, bf16[4,2048,128]{2,1,0:T(8,128)(2,1)} %get-tuple-element.128, f32[4,512]{1,0:T(4,128)S(1)} %fusion.111, f32[4,512,2048]{2,1,0:T(8,128)} %fusion.110), kind=kOutput, calls=%fused_computation.13.clone.1 | convolution fusion | flops 1094979584 | bytes 36184576 | tf_op jit(solution)/shard_map/while/body/eval_jaxpr/pqk,pke->pqe/dot_general | solution.py:110
  812.2 3.4 copy.135
  815.6 52.2 %all_to_all.41 = bf16[4,2048,128]{2,0,1:T(4,128)(2,1)S(1)} all-to-all(bf16[4,2048,128]{2,0,1:T(4,128)(2,1)S(1)} %copy.135), channel_id=1, replica_groups=mesh['expert'=8,'rep'=4] {'expert'}, dimensions={1} | all-to-all | bytes 4194304 | tf_op jit(solution)/shard_map/all_to_all | solution.py:120
  868.3 3.6 bitcast_convert_fusion.1
  871.9 3.0 bitcast_convert_fusion.2
  875.0 1.3 bitcast_convert_fusion
  876.6 6.0 fusion.41
  882.6 3.5 copy.138
  886.1 4.3 reshape.213
  890.3 5.2 fusion.93
  895.5 2.4 fusion.62
  898.8 3.5 copy.139
  (88 shorter events, 11.3 us)
Async XLA Ops:
  7.2 888.3 %copy-start = (f32[1024]{0:T(1024)S(1)}, f32[1024]{0:T(1024)}, u32[]{:S(2)}) copy-start(f32[1024]{0:T(1024)} %param.27) | copy-start | bytes 12292
  7.2 178.8 %all-gather.8.cloned.1.call-start = ((), (), s32[]{:S(2)}) async-start(), calls=%async_computation.5 | async-start | bytes 14417920 | tf_op jit(solution)/shard_map/all_gather | solution.py:42
  7.9 192.8 %all-gather.6.cloned.1.call-start = ((), (), s32[]{:S(2)}) async-start(), calls=%async_computation.4 | async-start | bytes 14417920 | tf_op jit(solution)/shard_map/all_gather | solution.py:41
  8.7 235.2 %all-gather.10.cloned.1.call-start = ((), (), s32[]{:S(2)}) async-start(), calls=%async_computation.6 | async-start | bytes 14417920 | tf_op jit(solution)/shard_map/all_gather | solution.py:43
  9.4 446.3 %all-gather.12.cloned.1.call-start = ((), (), s32[]{:S(2)}) async-start(), calls=%async_computation.7 | async-start | bytes 31457280 | tf_op jit(solution)/shard_map/all_gather | solution.py:44
  20.2 0.7 copy-start.8
  20.2 6.9 copy-start.1
  33.3 17.2 %copy-start.9 = (f32[2048]{0:T(1024)S(1)}, f32[2048]{0:T(1024)}, u32[]{:S(2)}) copy-start(f32[2048]{0:T(1024)} %param.18) | copy-start | bytes 24580
  243.9 5.3 copy-start.13
  275.8 6.6 copy-start.10
  275.8 6.8 copy-start.11
  275.8 121.8 %all-to-all-start.1 = ((bf16[8,160,2048]{2,1,0:T(8,128)(2,1)}), bf16[8,160,2048]{2,1,0:T(8,128)(2,1)}, u32[]{:S(2)}, u32[]{:S(2)}) async-start(bf16[8,160,2048]{2,1,0:T(8,128)(2,1)} %bitcast.200), calls=%async_computation.1 | async-start | bytes 10485760 | tf_op jit(solution)/shard_map/all_to_all | solution.py:77
  444.1 6.0 copy-start.2
  450.1 5.7 copy-start.12
  482.3 8.3 copy-start.4
  510.7 142.5 %all-to-all-start.2 = ((bf16[3,32,256,128]{3,2,0,1:T(8,128)(2,1)}), bf16[3,32,256,128]{3,2,0,1:T(8,128)(2,1)}, u32[]{:S(2)}, u32[]{:S(2)}) async-start(bf16[3,32,256,128]{3,2,0,1:T(8,128)(2,1)} %pad_maximum_fusion), calls=%async_computation.2 | async-start | bytes 12582912 | tf_op jit(solution)/shard_map/all_to_all | solution.py:95
  515.6 352.6 %all-gather.14.cloned.1.call-start = ((), (), s32[]{:S(2)}) async-start(), calls=%async_computation.8 | async-start | bytes 10485760 | tf_op jit(solution)/shard_map/all_gather | solution.py:46
  868.2 6.8 copy-start.6
  868.3 6.7 copy-start.7
  871.9 4.4 copy-start.5
  875.0 1.6 copy-start.3
Sparse Core Ops, SparseCore 0:
  9.5 78.8 all-gather.7
  90.0 76.1 all-gather.5
  167.7 76.1 all-gather.9
  245.3 154.8 all-gather.11
  517.7 59.0 all-gather.13
where the time goes:
time: 918 us; the launch traced here: 909 us
  waiting for transfers between devices  276 us (30%)
  matrix products  204 us (22%)
  blocking collectives  181 us (20%)
  local copies, waits for them, and re-layouts  113 us (12%)
  other arithmetic  110 us (12%)
  between operations  14.4 us (2%)
  starting transfers between devices  10.9 us (1%)
    all_to_all x1, waiting for transfers between devices, local(): lax.all_to_all(grouped, 'expert', split_axis=1, concat_axis=2, tiled=True)  137 us
    all_to_all x1, blocking collectives, local(): lax.all_to_all(outgoing, 'expert', split_axis=0, concat_axis=0, tiled=True)  123 us
    all_to_all x1, waiting for transfers between devices, local(): lax.all_to_all(results, 'expert', split_axis=0, concat_axis=0, tiled=True)  110 us
    dot_general x4, matrix products, attend(): jnp.einsum('pqk,pke->pqe', probs, value_rows, preferred_element_type=jnp....  58.9 us
    sub x4, other arithmetic, attend(): scores = scores - jnp.max(scores, axis=-1, keepdims=True)  56.5 us
    all_to_all x1, blocking collectives, local(): lax.all_to_all(attended, 'expert', split_axis=1, concat_axis=0, tiled=True)  52.2 us
    dot_general x4, matrix products, attend(): jnp.einsum('pqe,pke->pqk', query_block, key_rows, preferred_element_type=...  36.5 us
    dot_general x4, matrix products, local(): jnp.einsum('sjcf,jfd->sjcd', hidden[..., low:low + ff_part], down_full[:,...  29 us
  transfers between devices with their start and end apart: 7, of which 3 were waited for; matrix products, arithmetic and copies ran while one was open for 37% of the time, Pallas kernels for 0%

commit v1 on v0

--- a/solution.py
+++ b/solution.py
@@ -40,7 +40,25 @@
     capacity = max(2, tok_count * 10 // (4 * expert_total))
     gate_full = lax.all_gather(expert_gate, "rep", axis=2, tiled=True)
     up_full = lax.all_gather(expert_up, "rep", axis=2, tiled=True)
-    down_full = lax.all_gather(expert_down, "rep", axis=1, tiled=True)
+    size, index, rows = (lax.axis_size("rep"), lax.axis_index("rep"), expert_down.shape[1])
+    right = [(i, (i + 1) % size) for i in range(size)]
+    left = [(i, (i - 1) % size) for i in range(size)]
+    down_full = jnp.zeros(
+        (*expert_down.shape[:1], size * rows, *expert_down.shape[1 + 1 :]), expert_down.dtype
+    )
+    down_full = lax.dynamic_update_slice_in_dim(down_full, expert_down, index * rows, axis=1)
+    from_left = from_right = expert_down
+    half = size // 2
+    for step in range(1, half + 1):
+        from_left = lax.ppermute(from_left, "rep", right)
+        down_full = lax.dynamic_update_slice_in_dim(
+            down_full, from_left, (index - step) % size * rows, axis=1
+        )
+        if step < size - half:
+            from_right = lax.ppermute(from_right, "rep", left)
+            down_full = lax.dynamic_update_slice_in_dim(
+                down_full, from_right, (index + step) % size * rows, axis=1
+            )
     qkv_full = lax.all_gather(teacher_qkv, "rep", axis=2, tiled=True)
     qk_gain_full = lax.all_gather(qk_gain, "rep", axis=1, tiled=True)
     out_full = lax.all_gather(teacher_out, "rep", axis=0, tiled=True)

time: 918 us -> 951 us (1.036)
  waiting for transfers between devices: 276 us -> 400 us
  blocking collectives: 181 us -> 57.6 us
  local copies, waits for them, and re-layouts: 113 us -> 132 us
    ppermute x0 -> x3, waiting for transfers between devices: none -> 153 us  [the longest x2 153 us: local(): from_left = lax.ppermute(from_left, 'rep', right)]
    all_to_all x1 -> x0, blocking collectives: 123 us -> none  [local(): lax.all_to_all(outgoing, 'expert', split_axis=0, concat_axis=0, tiled=True)]
    all_gather x1 -> x0, waiting for transfers between devices: 26.6 us -> none  [local(): down_full = lax.all_gather(expert_down, 'rep', axis=1, tiled=True)]
    dynamic_update_slice x0 -> x4, local copies, waits for them, and re-layouts: none -> 14.2 us  [the longest x2 8.58 us: local(): lax.dynamic_update_slice_in_dim(down_full, from_left, (index - step) % si...]
  transfers between devices with their start and end apart: 7 -> 10, of which waited for: 3 -> 4; matrix products, arithmetic and copies ran while one was open for 37% -> 38% of each run, Pallas kernels for 0% -> 0%
where the time goes in v1:
time: 951 us; the launch traced here: 943 us
  waiting for transfers between devices  400 us (42%)
  matrix products  204 us (21%)
  local copies, waits for them, and re-layouts  132 us (14%)
  other arithmetic  114 us (12%)
  blocking collectives  57.6 us (6%)
  starting transfers between devices  20.4 us (2%)
  between operations  14.5 us (2%)
    ppermute x2, waiting for transfers between devices, local(): from_left = lax.ppermute(from_left, 'rep', right)  153 us
    all_to_all x1, waiting for transfers between devices, local(): lax.all_to_all(grouped, 'expert', split_axis=1, concat_axis=2, tiled=True)  136 us
    all_to_all x1, waiting for transfers between devices, local(): lax.all_to_all(results, 'expert', split_axis=0, concat_axis=0, tiled=True)  109 us
    dot_general x4, matrix products, attend(): jnp.einsum('pqk,pke->pqe', probs, value_rows, preferred_element_type=jnp....  58.9 us
    sub x4, other arithmetic, attend(): scores = scores - jnp.max(scores, axis=-1, keepdims=True)  58.3 us
    all_to_all x1, blocking collectives, local(): lax.all_to_all(attended, 'expert', split_axis=1, concat_axis=0, tiled=True)  52.2 us
    dot_general x4, matrix products, attend(): jnp.einsum('pqe,pke->pqk', query_block, key_rows, preferred_element_type=...  36.8 us
    dot_general x4, matrix products, local(): jnp.einsum('sjcf,jfd->sjcd', hidden[..., low:low + ff_part], down_full[:,...  27.8 us
  transfers between devices with their start and end apart: 10, of which 4 were waited for; matrix products, arithmetic and copies ran while one was open for 38% of the time, Pallas kernels for 0%

profile of v1, /device:TPU:0, one launch (start us, length us, event | category | flops | bytes accessed | tf_op | source)
XLA Modules:
  0.0 942.6 jit_solution(1703464063962287516)
XLA Ops:
  8.7 10.7 %copy.124 = bf16[2048,3,4,128]{0,3,2,1:T(8,128)(2,1)} copy(bf16[2048,3,4,128]{3,2,1,0:T(4,128)(2,1)} %param.23) | data formatting | bytes 12582912 | tf_op args[8]
  21.0 4.5 reduce-window.6
  27.3 5.2 copy.115
  32.5 6.0 reshape.216
  40.2 4.5 scatter_custom_fusion.1
  44.8 4.3 scatter_custom_fusion
  51.8 6.1 gather_fusion
  57.9 6.0 select_select_fusion
  64.0 7.6 all-to-all-start
  73.4 108.6 %collective-permute-done = bf16[2,352,2048]{2,1,0:T(8,128)(2,1)} collective-permute-done((bf16[2,352,2048]{2,1,0:T(8,128)(2,1)S(1)}, bf16[2,352,2048]{2,1,0:T(8,128)(2,1)}, u32[]{:S(2)}, u32[]{:S(2)}) %collective-permute-start) | collective-permute-done | bytes 2883616 | tf_op jit(solution)/shard_map/ppermute | solution.py:53
  182.0 5.7 broadcast_in_dim.70
  189.5 3.8 constant_dynamic-update-slice_fusion.2
  193.3 3.8 constant_dynamic-update-slice_fusion.1
  197.1 44.0 %collective-permute-done.2 = bf16[2,352,2048]{2,1,0:T(8,128)(2,1)} collective-permute-done((bf16[2,352,2048]{2,1,0:T(8,128)(2,1)}, bf16[2,352,2048]{2,1,0:T(8,128)(2,1)}, u32[]{:S(2)}, u32[]{:S(2)}) %collective-permute-start.2) | collective-permute-done | bytes 2883616 | tf_op jit(solution)/shard_map/ppermute | solution.py:53
  241.1 4.8 constant_dynamic-update-slice_fusion
  245.9 15.8 %fusion.23 = f32[2,8,80,1408]{3,2,1,0:T(8,128)} fusion(bf16[2,2048,1408]{1,2,0:T(8,128)(2,1)} %all-gather.7.cloned.1.call-done, bf16[8,2,80,2048]{3,2,1,0:T(8,128)(2,1)} %bitcast.10), kind=kOutput, calls=%fused_computation.23 | convolution fusion | flops 7381975040 | bytes 23986176 | tf_op jit(solution)/shard_map/sjcd,jdf->sjcf/dot_general | solution.py:81
  261.7 16.4 %fusion.27 = bf16[8,2,80,1408]{3,2,0,1:T(8,128)(2,1)} fusion(f32[2,8,80,1408]{3,2,1,0:T(8,128)} %fusion.23, bf16[2,2048,1408]{1,2,0:T(8,128)(2,1)} %all-gather.5.cloned.1.call-done, bf16[8,2,80,2048]{3,2,1,0:T(8,128)(2,1)} %bitcast.10), kind=kOutput, calls=%fused_computation.31 | convolution fusion | flops 7392788480 | bytes 27590656 | tf_op jit(solution)/shard_map/sjcd,jdf->sjcf/dot_general | solution.py:80
  278.1 5.3 fusion.46
  283.4 6.5 fusion.45
  289.9 6.9 fusion.44
  296.8 9.2 fusion.31
  306.0 2.7 copy.119
  308.7 5.7 all-to-all-start.1
  315.5 5.4 all_gather.18
  320.9 108.9 %all-to-all-done.1 = bf16[8,160,2048]{2,1,0:T(8,128)(2,1)} async-done(((bf16[8,160,2048]{2,1,0:T(8,128)(2,1)}), bf16[8,160,2048]{2,1,0:T(8,128)(2,1)}, u32[]{:S(2)}, u32[]{:S(2)}) %all-to-all-start.1) | async-done | bytes 5242912 | tf_op jit(solution)/shard_map/all_to_all | solution.py:95
  429.8 12.2 %gather_fusion.1 = bf16[1024,2048]{1,0:T(8,128)(2,1)} fusion(bf16[1280,2048]{1,0:T(8,128)(2,1)} %bitcast.25, s32[1024]{0:T(1024)S(1)} %broadcast_clamp_fusion), kind=kCustom, calls=%fused_computation.1 | custom fusion | bytes 8392704 | tf_op jit(solution)/shard_map/jit(_take)/gather | solution.py:98
  442.0 7.6 gather.15
  449.6 20.7 %multiply_reduce_fusion.1 = f32[512,2048]{1,0:T(8,128)} fusion(bf16[512,2,2048]{2,1,0:T(2,128)(2,1)} %gather.15, pred[512,2]{1,0:T(8,128)(4,1)S(1)} %copy.113, f32[512,2]{1,0:T(8,128)S(1)} %bitcast.213), kind=kLoop, calls=%fused_computation.28 | loop fusion | flops 7340032 | bytes 8393728 | tf_op jit(solution)/shard_map/reduce_sum | solution.py:99
  470.3 5.9 reduce_sum.77
  476.1 6.0 reduce_sum.76
  482.2 5.6 multiply_reduce_fusion.4
  487.8 26.4 %fusion.36 = f32[3,2,16,256,128]{3,4,2,0,1:T(8,128)} fusion(bf16[2048,3,16,128]{0,3,2,1:T(8,128)(2,1)} %all-gather.9.cloned.1.call-done, f32[2048]{0:T(1024)S(1)} %copy-done.13, f32[256,2]{0,1:T(2,128)S(1)} %add_rsqrt_fusion.2, f32[256,2,2048]{2,1,0:T(2,128)} %reduce_sum.76, bf16[1,256,2,2048]{3,2,1,0:T(2,128)(2,1)S(1)} %copy-done.2), kind=kOutput, calls=%fused_computation.44 | convolution fusion | flops 12892241920 | bytes 44050432 | tf_op jit(solution)/shard_map/sid,djhe->jihse/dot_general | solution.py:105
  514.2 4.8 multiply_reduce_fusion.3
  519.1 3.2 slice.165
  522.5 2.6 multiply_convert_fusion.1
  525.2 4.1 copy.126
  529.2 4.1 copy.127
  533.3 2.8 copy.128
  536.1 6.4 pad_maximum_fusion
  542.6 5.2 all-to-all-start.2
  548.3 136.4 %all-to-all-done.2 = bf16[3,32,256,128]{3,2,0,1:T(8,128)(2,1)} async-done(((bf16[3,32,256,128]{3,2,0,1:T(8,128)(2,1)}), bf16[3,32,256,128]{3,2,0,1:T(8,128)(2,1)}, u32[]{:S(2)}, u32[]{:S(2)}) %all-to-all-start.2) | async-done | bytes 6291488 | tf_op jit(solution)/shard_map/all_to_all | solution.py:113
  684.7 3.2 copy.129
  691.6 154.0 %while.10 = (s32[]{:T(128)}, bf16[4,4,512,128]{3,2,0,1:T(8,128)(2,1)}, bf16[4,4,512,128]{3,2,0,1:T(8,128)(2,1)}, bf16[4,2048,128]{2,1,0:T(8,128)(2,1)S(1)}, bf16[4,2048,128]{2,1,0:T(8,128)(2,1)}, /*index=5*/s32[]{:T(128)}) while((s32[]{:T(128)}, bf16[4,4,512,128]{3,2,0,1:T(8,128)(2,1)}, bf16[4,4,512,128]{3,2,0,1:T(8,128)(2,1)}, ...), condition=%wide.region_13.14_spmd, body=%wide.region_10.13_spmd.sunk | while | flops 2185500672 | bytes 72369224 | solution.py:136
  691.6 9.2 fusion.110
  700.8 14.6 %fusion.111 = f32[4,512]{1,0:T(4,128)S(1)} fusion(f32[4,512,2048]{2,1,0:T(8,128)} %fusion.110), kind=kOutput, calls=%fused_computation.139.clone.1 | output fusion | flops 16779264 | bytes 16785408 | tf_op jit(solution)/shard_map/while/body/eval_jaxpr/sub | solution.py:125
  715.4 14.7 %fusion.112 = bf16[4,4,512,128]{3,2,0,1:T(8,128)(2,1)} fusion(bf16[4,4,512,128]{3,2,0,1:T(8,128)(2,1)} %get-tuple-element.119, s32[]{:T(128)} %get-tuple-element.118, bf16[4,2048,128]{2,1,0:T(8,128)(2,1)} %get-tuple-element.128, f32[4,512]{1,0:T(4,128)S(1)} %fusion.111, f32[4,512,2048]{2,1,0:T(8,128)} %fusion.110), kind=kOutput, calls=%fused_computation.13.clone.1 | convolution fusion | flops 1094979584 | bytes 36184576 | tf_op jit(solution)/shard_map/while/body/eval_jaxpr/pqk,pke->pqe/dot_general | solution.py:128
  730.1 9.2 fusion.110
  739.3 14.6 %fusion.111 = f32[4,512]{1,0:T(4,128)S(1)} fusion(f32[4,512,2048]{2,1,0:T(8,128)} %fusion.110), kind=kOutput, calls=%fused_computation.139.clone.1 | output fusion | flops 16779264 | bytes 16785408 | tf_op jit(solution)/shard_map/while/body/eval_jaxpr/sub | solution.py:125
  753.9 14.7 %fusion.112 = bf16[4,4,512,128]{3,2,0,1:T(8,128)(2,1)} fusion(bf16[4,4,512,128]{3,2,0,1:T(8,128)(2,1)} %get-tuple-element.119, s32[]{:T(128)} %get-tuple-element.118, bf16[4,2048,128]{2,1,0:T(8,128)(2,1)} %get-tuple-element.128, f32[4,512]{1,0:T(4,128)S(1)} %fusion.111, f32[4,512,2048]{2,1,0:T(8,128)} %fusion.110), kind=kOutput, calls=%fused_computation.13.clone.1 | convolution fusion | flops 1094979584 | bytes 36184576 | tf_op jit(solution)/shard_map/while/body/eval_jaxpr/pqk,pke->pqe/dot_general | solution.py:128
  768.7 9.2 fusion.110
  777.9 14.6 %fusion.111 = f32[4,512]{1,0:T(4,128)S(1)} fusion(f32[4,512,2048]{2,1,0:T(8,128)} %fusion.110), kind=kOutput, calls=%fused_computation.139.clone.1 | output fusion | flops 16779264 | bytes 16785408 | tf_op jit(solution)/shard_map/while/body/eval_jaxpr/sub | solution.py:125
  792.4 14.7 %fusion.112 = bf16[4,4,512,128]{3,2,0,1:T(8,128)(2,1)} fusion(bf16[4,4,512,128]{3,2,0,1:T(8,128)(2,1)} %get-tuple-element.119, s32[]{:T(128)} %get-tuple-element.118, bf16[4,2048,128]{2,1,0:T(8,128)(2,1)} %get-tuple-element.128, f32[4,512]{1,0:T(4,128)S(1)} %fusion.111, f32[4,512,2048]{2,1,0:T(8,128)} %fusion.110), kind=kOutput, calls=%fused_computation.13.clone.1 | convolution fusion | flops 1094979584 | bytes 36184576 | tf_op jit(solution)/shard_map/while/body/eval_jaxpr/pqk,pke->pqe/dot_general | solution.py:128
  807.2 9.2 fusion.110
  816.4 14.6 %fusion.111 = f32[4,512]{1,0:T(4,128)S(1)} fusion(f32[4,512,2048]{2,1,0:T(8,128)} %fusion.110), kind=kOutput, calls=%fused_computation.139.clone.1 | output fusion | flops 16779264 | bytes 16785408 | tf_op jit(solution)/shard_map/while/body/eval_jaxpr/sub | solution.py:125
  830.9 14.7 %fusion.112 = bf16[4,4,512,128]{3,2,0,1:T(8,128)(2,1)} fusion(bf16[4,4,512,128]{3,2,0,1:T(8,128)(2,1)} %get-tuple-element.119, s32[]{:T(128)} %get-tuple-element.118, bf16[4,2048,128]{2,1,0:T(8,128)(2,1)} %get-tuple-element.128, f32[4,512]{1,0:T(4,128)S(1)} %fusion.111, f32[4,512,2048]{2,1,0:T(8,128)} %fusion.110), kind=kOutput, calls=%fused_computation.13.clone.1 | convolution fusion | flops 1094979584 | bytes 36184576 | tf_op jit(solution)/shard_map/while/body/eval_jaxpr/pqk,pke->pqe/dot_general | solution.py:128
  845.7 3.4 copy.135
  849.1 52.2 %all_to_all.40 = bf16[4,2048,128]{2,0,1:T(4,128)(2,1)S(1)} all-to-all(bf16[4,2048,128]{2,0,1:T(4,128)(2,1)S(1)} %copy.135), channel_id=1, replica_groups=mesh['expert'=8,'rep'=4] {'expert'}, dimensions={1} | all-to-all | bytes 4194304 | tf_op jit(solution)/shard_map/all_to_all | solution.py:138
  901.8 3.6 bitcast_convert_fusion.1
  905.5 3.0 bitcast_convert_fusion.2
  910.1 6.0 fusion.41
  916.1 3.5 copy.138
  919.6 4.3 reshape.213
  923.9 5.2 fusion.93
  932.3 3.5 copy.139
  (99 shorter events, 23.7 us)
Async XLA Ops:
  7.2 921.9 %copy-start = (f32[1024]{0:T(1024)S(1)}, f32[1024]{0:T(1024)}, u32[]{:S(2)}) copy-start(f32[1024]{0:T(1024)} %param.27) | copy-start | bytes 12292
  7.2 238.7 %all-gather.7.cloned.1.call-start = ((), (), s32[]{:S(2)}) async-start(), calls=%async_computation.5 | async-start | bytes 14417920 | tf_op jit(solution)/shard_map/all_gather | solution.py:42
  7.9 253.8 %all-gather.5.cloned.1.call-start = ((), (), s32[]{:S(2)}) async-start(), calls=%async_computation.4 | async-start | bytes 14417920 | tf_op jit(solution)/shard_map/all_gather | solution.py:41
  8.7 479.1 %all-gather.9.cloned.1.call-start = ((), (), s32[]{:S(2)}) async-start(), calls=%async_computation.6 | async-start | bytes 31457280 | tf_op jit(solution)/shard_map/all_gather | solution.py:62
  19.4 0.7 copy-start.9
  19.4 6.9 copy-start.1
  32.5 16.7 %copy-start.10 = (f32[2048]{0:T(1024)S(1)}, f32[2048]{0:T(1024)}, u32[]{:S(2)}) copy-start(f32[2048]{0:T(1024)} %param.18) | copy-start | bytes 24580
  64.0 7.6 copy-start.7
  64.0 181.9 %all-to-all-start = ((bf16[8,160,2048]{2,1,0:T(8,128)(2,1)}), bf16[8,160,2048]{2,1,0:T(8,128)(2,1)}, u32[]{:S(2)}, u32[]{:S(2)}) async-start(bf16[8,160,2048]{2,1,0:T(8,128)(2,1)} %select_select_fusion), calls=%async_computation | async-start | bytes 10485760 | tf_op jit(solution)/shard_map/all_to_all | solution.py:78
  71.6 110.4 %collective-permute-start = (bf16[2,352,2048]{2,1,0:T(8,128)(2,1)S(1)}, bf16[2,352,2048]{2,1,0:T(8,128)(2,1)}, u32[]{:S(2)}, u32[]{:S(2)}) collective-permute-start(bf16[2,352,2048]{2,1,0:T(8,128)(2,1)S(1)} %copy-done.7), channel_id=1, source_target_pairs={{0,1},{1,2},{2,3},{3,0},{4,5},{5,6},{6,7},{7,4},{8,9},{9,10},{10,1... | collective-permute-start | bytes 8650760 | tf_op jit(solution)/shard_map/ppermute | solution.py:53
  71.7 121.7 %collective-permute-start.1 = (bf16[2,352,2048]{2,1,0:T(8,128)(2,1)S(1)}, bf16[2,352,2048]{2,1,0:T(8,128)(2,1)}, u32[]{:S(2)}, u32[]{:S(2)}) collective-permute-start(bf16[2,352,2048]{2,1,0:T(8,128)(2,1)S(1)} %copy-done.7), channel_id=1, source_target_pairs={{0,3},{1,0},{2,1},{3,2},{4,7},{5,4},{6,5},{7,6},{8,11},{9,8},{10,9... | collective-permute-start | bytes 8650760 | tf_op jit(solution)/shard_map/ppermute | solution.py:58
  182.0 59.1 %collective-permute-start.2 = (bf16[2,352,2048]{2,1,0:T(8,128)(2,1)}, bf16[2,352,2048]{2,1,0:T(8,128)(2,1)}, u32[]{:S(2)}, u32[]{:S(2)}) collective-permute-start(bf16[2,352,2048]{2,1,0:T(8,128)(2,1)} %collective-permute-done), channel_id=1, source_target_pairs={{0,1},{1,2},{2,3},{3,0},{4,5},{5,6},{6,7},{7,4},{8,9},{9,10},{10,1... | collective-permute-start | bytes 8650760 | tf_op jit(solution)/shard_map/ppermute | solution.py:53
  278.1 5.3 copy-start.14
  308.7 6.5 copy-start.11
  308.7 6.7 copy-start.12
  308.7 121.1 %all-to-all-start.1 = ((bf16[8,160,2048]{2,1,0:T(8,128)(2,1)}), bf16[8,160,2048]{2,1,0:T(8,128)(2,1)}, u32[]{:S(2)}, u32[]{:S(2)}) async-start(bf16[8,160,2048]{2,1,0:T(8,128)(2,1)} %bitcast.200), calls=%async_computation.1 | async-start | bytes 10485760 | tf_op jit(solution)/shard_map/all_to_all | solution.py:95
  476.1 6.0 copy-start.2
  482.2 5.7 copy-start.13
  514.2 8.3 copy-start.4
  542.6 142.1 %all-to-all-start.2 = ((bf16[3,32,256,128]{3,2,0,1:T(8,128)(2,1)}), bf16[3,32,256,128]{3,2,0,1:T(8,128)(2,1)}, u32[]{:S(2)}, u32[]{:S(2)}) async-start(bf16[3,32,256,128]{3,2,0,1:T(8,128)(2,1)} %pad_maximum_fusion), calls=%async_computation.2 | async-start | bytes 12582912 | tf_op jit(solution)/shard_map/all_to_all | solution.py:113
  547.7 354.1 %all-gather.11.cloned.1.call-start = ((), (), s32[]{:S(2)}) async-start(), calls=%async_computation.7 | async-start | bytes 10485760 | tf_op jit(solution)/shard_map/all_gather | solution.py:64
  901.8 6.8 copy-start.6
  901.8 6.7 copy-start.8
  905.5 4.4 copy-start.5
  908.5 1.6 copy-start.3
Sparse Core Ops, SparseCore 0:
  9.5 90.3 all-gather.6
  101.5 122.8 all-gather.4
  226.0 154.8 all-gather.8
  549.8 59.4 all-gather.10
